TPU v7x, 32 devices: a whole 2x2x4 slice. The times are simulated.
32 devices in a mesh: ctx: 8 (over z, y), ch: 4 (over x, core).
Axes of the slice: x: 2, y: 2, z: 4, core: 2. Of those that a mesh axis runs over, the one named last changes fastest.
Arguments:
- projected: bfloat16 [3, 8192, 4096], P(None, 'ctx', 'ch'), may hold values from -6 to 6
- tap_weights: bfloat16 [3, 3, 4096], P(None, None, 'ch'), may hold values from -3.59375 to 3.59375
- pole_rates: float32 [16, 4096], P(None, 'ch'), may hold values from 1.2207031e-05 to 0.0625
- residues: float32 [16, 4096], P(None, 'ch'), may hold values from -1.4143862 to 1.4143862
- long_bias: float32 [4096], P('ch'), may hold values from -4 to 4
- out_weight: bfloat16 [4096, 4096], P(None, 'ch'), may hold values from -0.09375 to 0.09375
Outputs:
- mixed_out: bfloat16 [8192, 4096], P('ctx', 'ch')
All inputs are finite; a program needn't handle non-finite values.
Results may differ from a plain program's by a relative error of at most 0.012.
Values may be sent and summed in bfloat16 or wider, within the bound.
No kernel may reach another device: no remote copies, remote signals or barrier semaphores. Data moves between devices by JAX's collectives and lax.ppermute only.
A program may use at most 256 MiB of HBM per device.

v0:
```python
import jax
import jax.numpy as jnp
from jax import lax
from jax.sharding import PartitionSpec as P

BLOCK = 64


def shifted(value, axis, steps):
    count = lax.axis_size(axis)
    initial, last = (max(0, -steps), min(count, count - steps))
    return lax.ppermute(value, axis, [(source, source + steps) for source in range(initial, last)])


def make_tables(pole_rates, residues, block_size):
    lag_steps = jnp.arange(block_size, dtype=jnp.float32)
    powers = jnp.exp(-pole_rates[None, :, :] * lag_steps[:, None, None])
    kernel = jnp.sum(powers * residues[None, :, :], axis=1)
    offsets = (
        jnp.arange(block_size, dtype=jnp.int32)[:, None]
        - jnp.arange(block_size, dtype=jnp.int32)[None, :]
    )
    toeplitz = jnp.where(
        (offsets >= 0)[:, :, None], kernel[jnp.maximum(offsets, 0)], jnp.float32(0.0)
    )
    end_weights = powers[::-1]
    read_weights = powers * jnp.exp(-pole_rates)[None, :, :] * residues[None, :, :]
    block_decay = jnp.exp(-pole_rates * block_size)
    return (toeplitz, end_weights, read_weights, block_decay)


def combine(earlier, latter):
    return (earlier[0] * latter[0], latter[0] * earlier[1] + latter[1])


def channel_conv(rows_last, pole_rates, residues):
    highest = lax.Precision.HIGHEST
    channel_count = rows_last.shape[0]
    length = rows_last.shape[1]
    block_count = length // BLOCK
    pole_count = pole_rates.shape[0]
    toeplitz, end_weights, read_weights, block_decay = make_tables(pole_rates, residues, BLOCK)
    toeplitz_c = jnp.transpose(toeplitz, (2, 0, 1))
    blocks = rows_last.astype(jnp.float32).reshape(channel_count, block_count, BLOCK)
    inner_part = jnp.einsum("cij,cnj->cni", toeplitz_c, blocks, precision=highest)
    closing = jnp.einsum("jpc,cnj->ncp", end_weights, blocks, precision=highest)
    closing = closing.reshape(block_count, channel_count * pole_count)
    decay_row = jnp.transpose(block_decay).reshape(1, channel_count * pole_count)
    decays = jnp.broadcast_to(decay_row, closing.shape)
    _, states = lax.associative_scan(combine, (decays, closing), axis=0)
    before_state = jnp.concatenate([jnp.zeros_like(states[:1]), states[:-1]], 0)
    before_state = before_state.reshape(block_count, channel_count, pole_count)
    carried = jnp.einsum("ipc,ncp->cni", read_weights, before_state, precision=highest)
    return (inner_part + carried).reshape(channel_count, length)


def shards(projected, tap_weights, pole_rates, residues, long_bias, out_weight):
    row_count = projected.shape[1]
    rim_rows = tap_weights.shape[0] - 1
    prior_rows = shifted(projected[:, row_count - rim_rows :], "ctx", 1)
    extended = jnp.concatenate([prior_rows, projected], 1)
    featured = jnp.zeros(projected.shape, jnp.float32)
    for tap_index in range(rim_rows + 1):
        lead_row = rim_rows - tap_index
        featured = featured + tap_weights[tap_index].astype(jnp.float32)[:, None, :] * extended[
            :, lead_row : lead_row + row_count
        ].astype(jnp.float32)
    mixed_input = (featured[1] * featured[2]).astype(jnp.bfloat16)
    channel_major = jnp.transpose(mixed_input)
    spread = lax.all_to_all(channel_major, "ctx", split_axis=0, concat_axis=1, tiled=True)
    share_width = spread.shape[0]
    first_channel = lax.axis_index("ctx") * share_width
    rates_here = lax.dynamic_slice_in_dim(pole_rates, first_channel, share_width, 1)
    residues_here = lax.dynamic_slice_in_dim(residues, first_channel, share_width, 1)
    long_part = channel_conv(spread, rates_here, residues_here).astype(jnp.bfloat16)
    returned = lax.all_to_all(long_part, "ctx", split_axis=1, concat_axis=0, tiled=True)
    long_mix = jnp.transpose(returned)
    gated_mix = featured[0] * (
        long_mix.astype(jnp.float32) + long_bias[None, :] * mixed_input.astype(jnp.float32)
    )
    gated_mix = gated_mix.astype(jnp.bfloat16)
    mixed_out = jnp.dot(
        lax.all_gather(gated_mix, "ch", axis=1, tiled=True),
        out_weight,
        preferred_element_type=jnp.float32,
    )
    return mixed_out.astype(jnp.bfloat16)


def solution(mesh):
    in_specs = (
        P(None, "ctx", "ch"),
        P(None, None, "ch"),
        P(None, "ch"),
        P(None, "ch"),
        P("ch"),
        P(None, "ch"),
    )
    out_specs = P("ctx", "ch")
    return jax.shard_map(shards, mesh=mesh, in_specs=in_specs, out_specs=out_specs, check_vma=False)
```

profile of v0, /device:TPU:0, one launch (start us, length us, event | category | flops | bytes accessed | tf_op | source)
XLA Modules:
  0.0 405.2 jit_solution(4329657434524788336)
XLA Ops:
  7.4 4.9 %collective-permute-start = (bf16[3,2,1024]{2,1,0:T(2,128)(2,1)S(1)}, bf16[3,2,1024]{2,1,0:T(2,128)(2,1)S(1)}, u32[]{:S(2)}, u32[]{:S(2)}) collective-permute-start(bf16[3,2,1024]{2,1,0:T(2,128)(2,1)S(1)} %slice.176), channel_id=1, source_target_pairs={{0,4},{4,8},{8,12},{12,16},{16,20},{20,24},{24,28},{1,5},{5,9},{9,... | collective-permute-start | bytes 36872 | tf_op jit(solution)/shard_map/ppermute | solution.py:12
  13.0 8.7 %copy.43 = bf16[3,1024,1024]{1,2,0:T(8,128)(2,1)} copy(bf16[3,1024,1024]{2,1,0:T(8,128)(2,1)} %param.6) | data formatting | bytes 12582912 | tf_op args[0]
  22.1 15.7 %multiply_add_fusion = f32[3,1024,1024]{1,2,0:T(8,128)S(1)} fusion(bf16[3,1024,1024]{1,2,0:T(8,128)(2,1)} %copy.43, bf16[3,2,1024]{1,2,0:T(8,128)(2,1)S(1)} %copy.44, f32[3,1024]{1,0:T(4,128)S(1)} %get-tuple-element.12, f32[3,1024]{1,0:T(4,128)S(1)} %get-tuple-element.13, f32[3,1024]{1,0:T(4,128)S(1)} %get-tuple-element.11), kind=kLoop, calls=%fused_computation.1 | loop fusion | flops 44040192 | bytes 18923520 | tf_op jit(solution)/shard_map/add | solution.py:65
  37.8 4.5 %copy-done = f32[3,1024,1024]{1,2,0:T(8,128)} copy-done((f32[3,1024,1024]{1,2,0:T(8,128)}, f32[3,1024,1024]{1,2,0:T(8,128)S(1)}, u32[]{:S(2)}) %copy-start) | copy-done | bytes 12582936
  44.3 4.9 %all-to-all-start = ((bf16[8,128,1024]{2,1,0:T(8,128)(2,1)}), bf16[8,128,1024]{2,1,0:T(8,128)(2,1)}, u32[]{:S(2)}, u32[]{:S(2)}) async-start(bf16[8,128,1024]{2,1,0:T(8,128)(2,1)} %bitcast.6), calls=%async_computation | async-start | bytes 4194304 | tf_op jit(solution)/shard_map/all_to_all | solution.py:70
  53.5 10.8 %gather_fusion = f32[4096,128]{1,0:T(8,128)S(1)} fusion(f32[64,128]{1,0:T(8,128)S(1)} %copy.49, s32[4096]{0:T(1024)S(1)} %broadcast_clamp_fusion), kind=kCustom, calls=%fused_computation | custom fusion | bytes 4210688 | tf_op jit(solution)/shard_map/gather | solution.py:24
  64.3 4.6 %copy.50 = f32[64,64,128]{1,0,2:T(8,128)} copy(f32[64,64,128]{2,1,0:T(8,128)S(1)} %bitcast.56) | data formatting | bytes 4194304 | tf_op jit(solution)/shard_map/gather | solution.py:24
  70.8 26.5 %all-to-all-done = bf16[8,128,1024]{2,1,0:T(8,128)(2,1)} async-done(((bf16[8,128,1024]{2,1,0:T(8,128)(2,1)}), bf16[8,128,1024]{2,1,0:T(8,128)(2,1)}, u32[]{:S(2)}, u32[]{:S(2)}) %all-to-all-start) | async-done | bytes 2097184 | tf_op jit(solution)/shard_map/all_to_all | solution.py:70
  97.3 3.9 copy.46
  101.2 3.8 copy.51
  105.0 3.0 fusion.25
  108.0 20.3 %slice.187 = f32[64,2048]{0,1:T(8,128)} slice(f32[128,2048]{0,1:T(8,128)S(1)} %bitcast.52), slice={[0:127:2], [0:2048:1]} | slice | bytes 1048576 | tf_op jit(solution)/shard_map/slice | solution.py:50
  128.3 21.9 %slice.188 = f32[64,2048]{0,1:T(8,128)} slice(f32[128,2048]{0,1:T(8,128)S(1)} %bitcast.53), slice={[1:128:2], [0:2048:1]} | slice | bytes 1048576 | tf_op jit(solution)/shard_map/slice | solution.py:50
  184.5 21.6 %slice.226 = f32[63,2048]{0,1:T(8,128)} slice(f32[128,2048]{0,1:T(8,128)S(1)} %bitcast.54), slice={[2:128:2], [0:2048:1]} | slice | bytes 1032192 | tf_op jit(solution)/shard_map/slice | solution.py:50
  220.8 2.7 pad.55
  225.6 4.6 %pad.116 = f32[128,2048]{1,0:T(8,128)} pad(f32[64,2048]{1,0:T(8,128)} %add.128, f32[]{:T(128)} %constant.5.clone.1), padding=1_0_1x0_0_0 | pad | bytes 1572868
  243.5 4.2 %fusion.4 = f32[128,128,64]{1,2,0:T(8,128)S(1)} fusion(bf16[128,128,64]{1,2,0:T(8,128)(2,1)S(1)} %copy.51, f32[64,64,128]{1,0,2:T(8,128)} %copy.50, pred[64,64]{1,0:T(8,128)(4,1)S(1)} %copy-done.8), kind=kOutput, calls=%fused_computation.12 | convolution fusion | flops 805830656 | bytes 8392704 | tf_op jit(solution)/shard_map/cij,cnj->cni/dot_general | solution.py:45
  247.7 7.8 %add_convert_fusion = bf16[128,128,64]{1,2,0:T(8,128)(2,1)S(1)} fusion(f32[128,128,64]{1,2,0:T(8,128)S(1)} %fusion.4, f32[128,128,16]{0,2,1:T(8,128)S(1)} %bitcast.59, f32[16,128]{0,1:T(8,128)S(1)} %copy-done.6, f32[16,128]{0,1:T(8,128)S(1)} %copy-done.5, f32[16,128]{0,1:T(8,128)S(1)} %copy-done.3), kind=kOutput, calls=%fused_computation.15 | convolution fusion | flops 203816960 | bytes 7364608 | tf_op jit(solution)/shard_map/ipc,ncp->cni/dot_general | solution.py:53
  255.6 3.3 copy.60
  258.8 52.0 %all_to_all.26 = bf16[128,8,1024]{0,2,1:T(8,128)(2,1)S(1)} all-to-all(bf16[128,8,1024]{0,2,1:T(8,128)(2,1)} %bitcast.58), channel_id=1, replica_groups=mesh['ctx'=8,'ch'=4] {'ctx'}, dimensions={1} | all-to-all | bytes 4194304 | tf_op jit(solution)/shard_map/all_to_all | solution.py:76
  313.1 5.4 %copy.61 = f32[8,128,1024]{2,1,0:T(8,128)} copy(f32[8,128,1024]{1,2,0:T(8,128)} %convert_bitcast_fusion) | data formatting | bytes 8388608 | tf_op jit(solution)/shard_map/convert_element_type | solution.py:79
  318.5 7.7 %fusion.3 = bf16[1024,1024]{0,1:T(8,128)(2,1)} fusion(f32[3,1024,1024]{1,2,0:T(8,128)} %copy-done, f32[8,128,1024]{2,1,0:T(8,128)} %copy.61, f32[1024]{0:T(1024)S(1)} %copy-done.9), kind=kLoop, calls=%fused_computation.10 | loop fusion | flops 7340032 | bytes 18878464 | tf_op jit(solution)/shard_map/convert_element_type | solution.py:81
  326.2 57.5 %all-gather.2.cloned.1.call-done = bf16[1024,4096]{0,1:T(8,128)(2,1)} async-done(((bf16[1024,1024]{0,1:T(8,128)(2,1)}), bf16[1024,4096]{0,1:T(8,128)(2,1)}) %all-gather.2.cloned.1.call-update) | async-done | bytes 8388624 | tf_op jit(solution)/shard_map/all_gather | solution.py:83
  383.7 14.7 %convolution_convert_fusion = bf16[1024,1024]{1,0:T(8,128)(2,1)} fusion(bf16[1024,4096]{0,1:T(8,128)(2,1)} %all-gather.2.cloned.1.call-done, bf16[4096,1024]{1,0:T(8,128)(2,1)} %param.11), kind=kOutput, calls=%fused_computation.19 | convolution fusion | flops 8590983168 | bytes 18874368 | tf_op jit(solution)/shard_map/dot_general | solution.py:82
  (107 shorter events, 76.7 us)
Async XLA Ops:
  7.4 14.3 %collective-permute-start = (bf16[3,2,1024]{2,1,0:T(2,128)(2,1)S(1)}, bf16[3,2,1024]{2,1,0:T(2,128)(2,1)S(1)}, u32[]{:S(2)}, u32[]{:S(2)}) collective-permute-start(bf16[3,2,1024]{2,1,0:T(2,128)(2,1)S(1)} %slice.176), channel_id=1, source_target_pairs={{0,4},{4,8},{8,12},{12,16},{16,20},{20,24},{24,28},{1,5},{5,9},{9,... | collective-permute-start | bytes 36872 | tf_op jit(solution)/shard_map/ppermute | solution.py:12
  37.8 4.5 %copy-start = (f32[3,1024,1024]{1,2,0:T(8,128)}, f32[3,1024,1024]{1,2,0:T(8,128)S(1)}, u32[]{:S(2)}) copy-start(f32[3,1024,1024]{1,2,0:T(8,128)S(1)} %multiply_add_fusion) | copy-start | bytes 37748740
  44.3 52.9 %all-to-all-start = ((bf16[8,128,1024]{2,1,0:T(8,128)(2,1)}), bf16[8,128,1024]{2,1,0:T(8,128)(2,1)}, u32[]{:S(2)}, u32[]{:S(2)}) async-start(bf16[8,128,1024]{2,1,0:T(8,128)(2,1)} %bitcast.6), calls=%async_computation | async-start | bytes 4194304 | tf_op jit(solution)/shard_map/all_to_all | solution.py:70
  49.2 334.5 %all-gather.2.cloned.1.call-start = ((), (), s32[]{:S(2)}) async-start(), calls=%async_computation.2 | async-start | bytes 10485760 | tf_op jit(solution)/shard_map/all_gather | solution.py:83
  50.1 3.4 copy-start.2
  50.2 3.3 copy-start.4
  70.8 89.6 %copy-start.7 = (f32[2048]{0:T(1024)}, f32[2048]{0:T(1024)S(1)}, u32[]{:S(2)}) copy-start(f32[2048]{0:T(1024)S(1)} %get-tuple-element.17) | copy-start | bytes 24580
  181.4 37.7 %slice-start = ((f32[64,2048]{1,0:T(8,128)}), f32[1,2048]{1,0:T(1,128)S(1)}, s32[]{:S(2)}) async-start(f32[64,2048]{1,0:T(8,128)} %multiply_add_fusion.1), calls=%async_computation.3 | async-start | bytes 16384 | tf_op jit(solution)/shard_map/slice | solution.py:50
  210.8 0.7 copy-start.1
  237.2 6.3 %copy-start.8 = (pred[64,64]{1,0:T(8,128)(4,1)S(1)}, pred[64,64]{1,0:T(8,128)(4,1)}, u32[]{:S(2)}) copy-start(pred[64,64]{1,0:T(8,128)(4,1)} %subtract_compare_fusion) | copy-start | bytes 12292
  243.5 4.2 %copy-start.3 = (f32[16,128]{0,1:T(8,128)S(1)}, f32[16,128]{0,1:T(8,128)}, u32[]{:S(2)}) copy-start(f32[16,128]{0,1:T(8,128)} %copy-done.2) | copy-start | bytes 24580
  243.5 4.2 %copy-start.5 = (f32[16,128]{0,1:T(8,128)S(1)}, f32[16,128]{0,1:T(8,128)}, u32[]{:S(2)}) copy-start(f32[16,128]{0,1:T(8,128)} %copy-done.4) | copy-start | bytes 24580
  243.5 4.2 %copy-start.6 = (f32[16,128]{0,1:T(8,128)S(1)}, f32[16,128]{0,1:T(8,128)}, u32[]{:S(2)}) copy-start(f32[16,128]{0,1:T(8,128)} %copy.59) | copy-start | bytes 24580
  313.1 5.4 %copy-start.9 = (f32[1024]{0:T(1024)S(1)}, f32[1024]{0:T(1024)}, u32[]{:S(2)}) copy-start(f32[1024]{0:T(1024)} %param.10) | copy-start | bytes 12292
Sparse Core Ops, SparseCore 0:
  326.3 57.3 all-gather.1
where the time goes:
time: 408 us; the launch traced here: 405 us
  local copies, waits for them, and re-layouts  157 us (38%)
  waiting for transfers between devices  84 us (21%)
  other arithmetic  59.2 us (15%)
  blocking collectives  52 us (13%)
  matrix products  29.6 us (7%)
  between operations  13.7 us (3%)
  starting transfers between devices  9.79 us (2%)
    slice x24, local copies, waits for them, and re-layouts, channel_conv(): _, states = lax.associative_scan(combine, (decays, closing), axis=0)  83.2 us
    all_gather x1, waiting for transfers between devices, shards(): lax.all_gather(gated_mix, 'ch', axis=1, tiled=True)  57.5 us
    all_to_all x1, blocking collectives, shards(): lax.all_to_all(long_part, 'ctx', split_axis=1, concat_axis=0, tiled=True)  52 us
    unnamed x26, local copies, waits for them, and re-layouts  27.2 us
    all_to_all x1, waiting for transfers between devices, shards(): lax.all_to_all(channel_major, 'ctx', split_axis=0, concat_axis=1, tiled=T...  26.5 us
    add x1, other arithmetic, shards(): featured + tap_weights[tap_index].astype(jnp.float32)[:, None, :] * exten...  15.7 us
    gather x2, local copies, waits for them, and re-layouts, make_tables(): kernel[jnp.maximum(offsets, 0)]  15.3 us
    dot_general x1, matrix products, shards(): jnp.dot(lax.all_gather(gated_mix, 'ch', axis=1, tiled=True), out_weight,...  14.7 us
  transfers between devices with their start and end apart: 3, of which 2 were waited for; matrix products, arithmetic and copies ran while one was open for 8% of the time, Pallas kernels for 0%

commit v1 on v0

--- a/solution.py
+++ b/solution.py
@@ -73,7 +73,10 @@
     rates_here = lax.dynamic_slice_in_dim(pole_rates, first_channel, share_width, 1)
     residues_here = lax.dynamic_slice_in_dim(residues, first_channel, share_width, 1)
     long_part = channel_conv(spread, rates_here, residues_here).astype(jnp.bfloat16)
-    returned = lax.all_to_all(long_part, "ctx", split_axis=1, concat_axis=0, tiled=True)
+    returned = jnp.concatenate(
+        lax.all_to_all(jnp.stack(jnp.split(long_part, lax.axis_size("ctx"), axis=1)), "ctx", 0, 0),
+        axis=0,
+    )
     long_mix = jnp.transpose(returned)
     gated_mix = featured[0] * (
         long_mix.astype(jnp.float32) + long_bias[None, :] * mixed_input.astype(jnp.float32)

time: 408 us -> 405 us (level)
    unnamed x26 -> x33, local copies, waits for them, and re-layouts: 27.2 us -> 27.4 us
where the time goes in v1:
time: 405 us; the launch traced here: 402 us
  local copies, waits for them, and re-layouts  155 us (38%)
  waiting for transfers between devices  84 us (21%)
  other arithmetic  56.9 us (14%)
  blocking collectives  51.8 us (13%)
  matrix products  30.6 us (8%)
  between operations  13.8 us (3%)
  starting transfers between devices  9.79 us (2%)
    slice x24, local copies, waits for them, and re-layouts, channel_conv(): _, states = lax.associative_scan(combine, (decays, closing), axis=0)  83.2 us
    all_gather x1, waiting for transfers between devices, shards(): lax.all_gather(gated_mix, 'ch', axis=1, tiled=True)  57.5 us
    all_to_all x1, blocking collectives, shards(): lax.all_to_all(jnp.stack(jnp.split(long_part, lax.axis_size('ctx'), axis=...  51.8 us
    unnamed x33, local copies, waits for them, and re-layouts  27.4 us
    all_to_all x1, waiting for transfers between devices, shards(): lax.all_to_all(channel_major, 'ctx', split_axis=0, concat_axis=1, tiled=T...  26.5 us
    add x1, other arithmetic, shards(): featured + tap_weights[tap_index].astype(jnp.float32)[:, None, :] * exten...  15.7 us
    gather x2, local copies, waits for them, and re-layouts, make_tables(): kernel[jnp.maximum(offsets, 0)]  15.3 us
    dot_general x1, matrix products, shards(): jnp.dot(lax.all_gather(gated_mix, 'ch', axis=1, tiled=True), out_weight,...  14.7 us
  transfers between devices with their start and end apart: 3, of which 2 were waited for; matrix products, arithmetic and copies ran while one was open for 8% of the time, Pallas kernels for 0%

profile of v1, /device:TPU:0, one launch (start us, length us, event | category | flops | bytes accessed | tf_op | source)
XLA Modules:
  0.0 402.3 jit_solution(9090954370749593440)
XLA Ops:
  7.4 4.9 %collective-permute-start = (bf16[3,2,1024]{2,1,0:T(2,128)(2,1)S(1)}, bf16[3,2,1024]{2,1,0:T(2,128)(2,1)S(1)}, u32[]{:S(2)}, u32[]{:S(2)}) collective-permute-start(bf16[3,2,1024]{2,1,0:T(2,128)(2,1)S(1)} %slice.176), channel_id=1, source_target_pairs={{0,4},{4,8},{8,12},{12,16},{16,20},{20,24},{24,28},{1,5},{5,9},{9,... | collective-permute-start | bytes 36872 | tf_op jit(solution)/shard_map/ppermute | solution.py:12
  13.0 8.7 %copy.54 = bf16[3,1024,1024]{1,2,0:T(8,128)(2,1)} copy(bf16[3,1024,1024]{2,1,0:T(8,128)(2,1)} %param.6) | data formatting | bytes 12582912 | tf_op args[0]
  22.1 15.7 %multiply_add_fusion = f32[3,1024,1024]{1,2,0:T(8,128)S(1)} fusion(bf16[3,1024,1024]{1,2,0:T(8,128)(2,1)} %copy.54, bf16[3,2,1024]{1,2,0:T(8,128)(2,1)S(1)} %copy.55, f32[3,1024]{1,0:T(4,128)S(1)} %get-tuple-element.12, f32[3,1024]{1,0:T(4,128)S(1)} %get-tuple-element.13, f32[3,1024]{1,0:T(4,128)S(1)} %get-tuple-element.11), kind=kLoop, calls=%fused_computation.1 | loop fusion | flops 44040192 | bytes 18923520 | tf_op jit(solution)/shard_map/add | solution.py:65
  37.8 4.5 %copy-done = f32[3,1024,1024]{1,2,0:T(8,128)} copy-done((f32[3,1024,1024]{1,2,0:T(8,128)}, f32[3,1024,1024]{1,2,0:T(8,128)S(1)}, u32[]{:S(2)}) %copy-start) | copy-done | bytes 12582936
  44.3 4.9 %all-to-all-start = ((bf16[8,128,1024]{2,1,0:T(8,128)(2,1)}), bf16[8,128,1024]{2,1,0:T(8,128)(2,1)}, u32[]{:S(2)}, u32[]{:S(2)}) async-start(bf16[8,128,1024]{2,1,0:T(8,128)(2,1)} %bitcast.6), calls=%async_computation | async-start | bytes 4194304 | tf_op jit(solution)/shard_map/all_to_all | solution.py:70
  53.5 10.8 %gather_fusion = f32[4096,128]{1,0:T(8,128)S(1)} fusion(f32[64,128]{1,0:T(8,128)S(1)} %copy.60, s32[4096]{0:T(1024)S(1)} %broadcast_clamp_fusion), kind=kCustom, calls=%fused_computation | custom fusion | bytes 4210688 | tf_op jit(solution)/shard_map/gather | solution.py:24
  64.3 4.6 %copy.61 = f32[64,64,128]{1,0,2:T(8,128)} copy(f32[64,64,128]{2,1,0:T(8,128)S(1)} %bitcast.86) | data formatting | bytes 4194304 | tf_op jit(solution)/shard_map/gather | solution.py:24
  70.8 26.5 %all-to-all-done = bf16[8,128,1024]{2,1,0:T(8,128)(2,1)} async-done(((bf16[8,128,1024]{2,1,0:T(8,128)(2,1)}), bf16[8,128,1024]{2,1,0:T(8,128)(2,1)}, u32[]{:S(2)}, u32[]{:S(2)}) %all-to-all-start) | async-done | bytes 2097184 | tf_op jit(solution)/shard_map/all_to_all | solution.py:70
  97.3 3.9 copy.57
  101.2 3.8 copy.62
  105.0 3.0 fusion.33
  108.0 20.3 %slice.187 = f32[64,2048]{0,1:T(8,128)} slice(f32[128,2048]{0,1:T(8,128)S(1)} %bitcast.82), slice={[0:127:2], [0:2048:1]} | slice | bytes 1048576 | tf_op jit(solution)/shard_map/slice | solution.py:50
  128.3 21.9 %slice.188 = f32[64,2048]{0,1:T(8,128)} slice(f32[128,2048]{0,1:T(8,128)S(1)} %bitcast.83), slice={[1:128:2], [0:2048:1]} | slice | bytes 1048576 | tf_op jit(solution)/shard_map/slice | solution.py:50
  184.5 21.6 %slice.226 = f32[63,2048]{0,1:T(8,128)} slice(f32[128,2048]{0,1:T(8,128)S(1)} %bitcast.84), slice={[2:128:2], [0:2048:1]} | slice | bytes 1032192 | tf_op jit(solution)/shard_map/slice | solution.py:50
  220.8 2.7 pad.55
  225.6 4.6 %pad.116 = f32[128,2048]{1,0:T(8,128)} pad(f32[64,2048]{1,0:T(8,128)} %add.128, f32[]{:T(128)} %constant.5.clone.1), padding=1_0_1x0_0_0 | pad | bytes 1572868
  243.5 4.2 %fusion.4 = f32[128,128,64]{1,2,0:T(8,128)S(1)} fusion(bf16[128,128,64]{1,2,0:T(8,128)(2,1)S(1)} %copy.62, f32[64,64,128]{1,0,2:T(8,128)} %copy.61, pred[64,64]{1,0:T(8,128)(4,1)S(1)} %copy-done.8), kind=kOutput, calls=%fused_computation.12 | convolution fusion | flops 805830656 | bytes 8392704 | tf_op jit(solution)/shard_map/cij,cnj->cni/dot_general | solution.py:45
  247.7 8.8 %add_convert_fusion = bf16[128,128,64]{1,2,0:T(8,128)(2,1)} fusion(f32[128,128,64]{1,2,0:T(8,128)S(1)} %fusion.4, f32[128,128,16]{0,2,1:T(8,128)S(1)} %bitcast.96, f32[16,128]{0,1:T(8,128)S(1)} %copy-done.6, f32[16,128]{0,1:T(8,128)S(1)} %copy-done.5, f32[16,128]{0,1:T(8,128)S(1)} %copy-done.3), kind=kOutput, calls=%fused_computation.14 | convolution fusion | flops 203816960 | bytes 7364608 | tf_op jit(solution)/shard_map/ipc,ncp->cni/dot_general | solution.py:53
  256.5 3.8 copy.71
  260.7 51.8 %all_to_all.21 = bf16[8,128,1024]{1,2,0:T(8,128)(2,1)S(1)} all-to-all(bf16[8,128,1024]{1,2,0:T(8,128)(2,1)S(1)} %fusion.15), channel_id=1, replica_groups=mesh['ctx'=8,'ch'=4] {'ctx'}, dimensions={0} | all-to-all | bytes 4194304 | tf_op jit(solution)/shard_map/all_to_all | solution.py:77
  312.5 3.1 copy.74
  315.6 7.7 %fusion.3 = bf16[1024,1024]{0,1:T(8,128)(2,1)} fusion(f32[3,1024,1024]{1,2,0:T(8,128)} %copy-done, f32[8,128,1024]{2,1,0:T(8,128)} %copy.74, f32[1024]{0:T(1024)S(1)} %copy-done.9), kind=kLoop, calls=%fused_computation.10 | loop fusion | flops 7340032 | bytes 18878464 | tf_op jit(solution)/shard_map/convert_element_type | solution.py:84
  323.3 57.5 %all-gather.2.cloned.1.call-done = bf16[1024,4096]{0,1:T(8,128)(2,1)} async-done(((bf16[1024,1024]{0,1:T(8,128)(2,1)}), bf16[1024,4096]{0,1:T(8,128)(2,1)}) %all-gather.2.cloned.1.call-update) | async-done | bytes 8388624 | tf_op jit(solution)/shard_map/all_gather | solution.py:86
  380.8 14.7 %convolution_convert_fusion = bf16[1024,1024]{1,0:T(8,128)(2,1)} fusion(bf16[1024,4096]{0,1:T(8,128)(2,1)} %all-gather.2.cloned.1.call-done, bf16[4096,1024]{1,0:T(8,128)(2,1)} %param.11), kind=kOutput, calls=%fused_computation.18 | convolution fusion | flops 8590983168 | bytes 18874368 | tf_op jit(solution)/shard_map/dot_general | solution.py:85
  (114 shorter events, 74.8 us)
Async XLA Ops:
  7.4 14.3 %collective-permute-start = (bf16[3,2,1024]{2,1,0:T(2,128)(2,1)S(1)}, bf16[3,2,1024]{2,1,0:T(2,128)(2,1)S(1)}, u32[]{:S(2)}, u32[]{:S(2)}) collective-permute-start(bf16[3,2,1024]{2,1,0:T(2,128)(2,1)S(1)} %slice.176), channel_id=1, source_target_pairs={{0,4},{4,8},{8,12},{12,16},{16,20},{20,24},{24,28},{1,5},{5,9},{9,... | collective-permute-start | bytes 36872 | tf_op jit(solution)/shard_map/ppermute | solution.py:12
  37.8 4.5 %copy-start = (f32[3,1024,1024]{1,2,0:T(8,128)}, f32[3,1024,1024]{1,2,0:T(8,128)S(1)}, u32[]{:S(2)}) copy-start(f32[3,1024,1024]{1,2,0:T(8,128)S(1)} %multiply_add_fusion) | copy-start | bytes 37748740
  44.3 52.9 %all-to-all-start = ((bf16[8,128,1024]{2,1,0:T(8,128)(2,1)}), bf16[8,128,1024]{2,1,0:T(8,128)(2,1)}, u32[]{:S(2)}, u32[]{:S(2)}) async-start(bf16[8,128,1024]{2,1,0:T(8,128)(2,1)} %bitcast.6), calls=%async_computation | async-start | bytes 4194304 | tf_op jit(solution)/shard_map/all_to_all | solution.py:70
  49.2 331.6 %all-gather.2.cloned.1.call-start = ((), (), s32[]{:S(2)}) async-start(), calls=%async_computation.2 | async-start | bytes 10485760 | tf_op jit(solution)/shard_map/all_gather | solution.py:86
  50.1 3.4 copy-start.2
  50.2 3.3 copy-start.4
  70.8 89.6 %copy-start.7 = (f32[2048]{0:T(1024)}, f32[2048]{0:T(1024)S(1)}, u32[]{:S(2)}) copy-start(f32[2048]{0:T(1024)S(1)} %get-tuple-element.17) | copy-start | bytes 24580
  181.4 37.7 %slice-start = ((f32[64,2048]{1,0:T(8,128)}), f32[1,2048]{1,0:T(1,128)S(1)}, s32[]{:S(2)}) async-start(f32[64,2048]{1,0:T(8,128)} %multiply_add_fusion.1), calls=%async_computation.3 | async-start | bytes 16384 | tf_op jit(solution)/shard_map/slice | solution.py:50
  210.8 0.7 copy-start.1
  237.2 6.3 %copy-start.8 = (pred[64,64]{1,0:T(8,128)(4,1)S(1)}, pred[64,64]{1,0:T(8,128)(4,1)}, u32[]{:S(2)}) copy-start(pred[64,64]{1,0:T(8,128)(4,1)} %subtract_compare_fusion) | copy-start | bytes 12292
  243.5 4.2 %copy-start.3 = (f32[16,128]{0,1:T(8,128)S(1)}, f32[16,128]{0,1:T(8,128)}, u32[]{:S(2)}) copy-start(f32[16,128]{0,1:T(8,128)} %copy-done.2) | copy-start | bytes 24580
  243.5 4.2 %copy-start.5 = (f32[16,128]{0,1:T(8,128)S(1)}, f32[16,128]{0,1:T(8,128)}, u32[]{:S(2)}) copy-start(f32[16,128]{0,1:T(8,128)} %copy-done.4) | copy-start | bytes 24580
  243.5 4.2 %copy-start.6 = (f32[16,128]{0,1:T(8,128)S(1)}, f32[16,128]{0,1:T(8,128)}, u32[]{:S(2)}) copy-start(f32[16,128]{0,1:T(8,128)} %copy.70) | copy-start | bytes 24580
  312.5 3.1 copy-start.9
Sparse Core Ops, SparseCore 0:
  323.4 57.3 all-gather.1
